TPU v7x, 512 devices: a whole 4x8x8 slice. The times are simulated.
512 devices in a mesh: tm: 64 (over z, x, y_hi), chan: 8 (over y_lo, core).
Axes of the slice: x: 4, y: 8 (y_hi: 2, y_lo: 4; y = y_hi * 4 + y_lo), z: 8, core: 2. Of those that a mesh axis runs over, the one named last changes fastest.
Arguments:
- field: float32 [2, 2, 64, 65536], P(None, None, 'chan', 'tm'), may hold values from -15.5 to 15.5
- noise: float32 [1, 2, 2, 64, 65536], P(None, None, None, 'chan', 'tm'), may hold values from -1.25 to 1.25
- assign: int32 [64], P('chan'), may hold values from 0 to 63, each once
Outputs:
- received: float32 [2, 2, 64, 65536], P(None, None, 'chan', 'tm')
- recovered: float32 [2, 2, 64, 65536], P(None, None, 'chan', 'tm')
All inputs are finite; a program needn't handle non-finite values.
Results may differ from a plain program's by a relative error of at most 0.0003.
Values sent between devices are 32-bit elements; how exact they have to be, the bound alone decides.
No kernel may reach another device: no remote copies, remote signals or barrier semaphores. Data moves between devices by JAX's collectives and lax.ppermute only.
A program may use at most 64 MiB of HBM per device.

v0:
```python
import jax
import jax.numpy as jnp
from jax import lax
from jax.sharding import Mesh, PartitionSpec as P

OPTICAL_CHANNELS = 64
FILTER_HALF_TAPS = 128
STEPS = 2
FIBER_SECTIONS = 1
ATT = 0.955
GAMMA = 0.004
WALK = 0.5
SPREAD = 0.4
CHIRP = 0.25
EPS = 1e-06


def tap_tables(channel_ids, sign, reach, channels):
    rows = jnp.arange(3 * reach, dtype=jnp.int32)[:, None]
    cols = jnp.arange(reach, dtype=jnp.int32)[None, :]
    lag = cols - rows + reach
    interior_part = (jnp.abs(lag) <= reach).astype(jnp.float32)
    centre = (
        WALK * reach * (2.0 * channel_ids.astype(jnp.float32) - (channels - 1)) / (channels - 1)
    )
    centre = centre[:, None, None]
    width = SPREAD * reach
    offset = sign * lag.astype(jnp.float32)[None] - centre
    symbol_profile = jnp.exp(-jnp.square(offset / width))
    turn = jnp.square(offset) / (2.0 * CHIRP * reach)
    taps = jnp.arange(-reach, reach + 1, dtype=jnp.int32).astype(jnp.float32)
    scale = jnp.sqrt(
        jnp.sum(jnp.exp(-2.0 * jnp.square((taps[None, :] - centre[:, :, 0]) / width)), axis=1)
    )
    scale = scale[:, None, None]
    mat_re = interior_part * symbol_profile * jnp.cos(turn) / scale
    mat_im = sign * interior_part * symbol_profile * jnp.sin(turn) / scale
    return (mat_re, mat_im)


def merged_table(mat_re, mat_im):
    top = jnp.concatenate([mat_re, mat_im], axis=2)
    bottom = jnp.concatenate([-mat_im, mat_re], axis=2)
    return jnp.concatenate([top, bottom], axis=1)


def disperse(ext, table, reach):
    pols, parts, chans, segment_length = ext.shape
    blocks = segment_length // reach - 2
    rows = ext.reshape(pols, parts, chans, blocks + 2, reach)
    window = jnp.concatenate(
        [rows[:, :, :, 0:blocks], rows[:, :, :, 1 : blocks + 1], rows[:, :, :, 2 : blocks + 2]],
        axis=4,
    )
    stacked = jnp.moveaxis(window, 1, 3).reshape(pols, chans, blocks, parts * 3 * reach)
    out = jnp.einsum("pcjq,cqn->pcjn", stacked, table, precision=lax.Precision.HIGHEST)
    out = jnp.moveaxis(out.reshape(pols, chans, blocks, parts, reach), 3, 1)
    return out.reshape(pols, parts, chans, blocks * reach)


def rotate(ext, sign, own, total):
    angle = sign * GAMMA * (2.0 * total[None, :] - own)
    cosine = jnp.cos(angle)
    sine = jnp.sin(angle)
    real = ext[:, 0]
    imag = ext[:, 1]
    return jnp.stack([real * cosine - imag * sine, real * sine + imag * cosine], axis=1)


TM = ("z", "x", "yh")
CHAN = ("ylo", "core")


def psum_tm(value):
    for axis in ("yh", "x", "z"):
        value = lax.psum(value, axis)
    return value


def psum_chan(value):
    for axis in ("core", "ylo"):
        value = lax.psum(value, axis)
    return value


def on_device(field, noise, assign):
    forward, backward = lax.optimization_barrier(
        (
            merged_table(*tap_tables(assign, 1.0, FILTER_HALF_TAPS, OPTICAL_CHANNELS)),
            merged_table(*tap_tables(assign, -1.0, FILTER_HALF_TAPS, OPTICAL_CHANNELS)),
        )
    )
    total_len = lax.axis_size(TM) * field.shape[3]
    reach = FILTER_HALF_TAPS
    field_width = 2 * STEPS * reach
    noise_width = STEPS * reach

    def nonlinear(ext, sign):
        own = jnp.sum(jnp.square(ext), axis=(0, 1))
        total = psum_chan(jnp.sum(own, axis=0))
        return rotate(ext, sign, own, total)

    last_noise = noise[FIBER_SECTIONS - 1]
    count, length = (lax.axis_size(TM), field.shape[3])
    up = [(i, (i + 1) % count) for i in range(count)]
    down = [(j, i) for i, j in up]
    trailing = jnp.concatenate(
        [field[..., length - field_width :], last_noise[..., length - noise_width :]], axis=3
    )
    leading = jnp.concatenate([field[..., :field_width], last_noise[..., :noise_width]], axis=3)
    before = lax.ppermute(trailing, TM, up)
    after = lax.ppermute(leading, TM, down)
    current = jnp.concatenate([before[..., :field_width], field, after[..., :field_width]], axis=3)
    noise_ext = jnp.concatenate(
        [before[..., field_width:], last_noise, after[..., field_width:]], axis=3
    )
    for step in range(STEPS):
        current = disperse(current, forward, reach) * ATT
        current = nonlinear(current, 1.0)
    centre = slice(noise_width, noise_width + length)
    signal, added = (current[..., centre], last_noise)
    sums = psum_tm(
        jnp.stack(
            [
                jnp.sum(jnp.square(signal), axis=(0, 1, 3)),
                jnp.sum(signal * added, axis=(0, 1, 3)),
                jnp.sum(jnp.square(added), axis=(0, 1, 3)),
            ]
        )
    )
    gain = lax.rsqrt(sums[0] / total_len + EPS)
    arrival = (gain * gain * sums[0] + 2.0 * gain * sums[1] + sums[2]) / total_len
    current = current * gain[None, None, :, None] + noise_ext
    received = current[..., centre]
    rescale = jnp.sqrt(ATT ** (2 * STEPS) / (arrival + EPS))
    current = current * rescale[None, None, :, None]
    for step in range(STEPS):
        current = nonlinear(current, -1.0) / ATT
        current = disperse(current, backward, reach)
    return (received, current)


def solution(mesh):
    tm, chan = (mesh.shape["tm"], mesh.shape["chan"])
    fine = Mesh(mesh.devices.reshape(tm // 16, 8, 2, chan // 2, 2), TM + CHAN)
    placed = (P(None, None, CHAN, TM), P(None, None, None, CHAN, TM), P(CHAN))
    return jax.shard_map(
        on_device,
        mesh=fine,
        in_specs=placed,
        out_specs=(P(None, None, CHAN, TM), P(None, None, CHAN, TM)),
        check_vma=False,
    )
```

profile of v0, /device:TPU:8, one launch (start us, length us, event | category | flops | bytes accessed | tf_op | source)
XLA Modules:
  0.0 157.8 jit_solution(16434985247068703220)
XLA Ops:
  0.6 0.0 copy-start.2
  0.6 0.8 fusion.85
  1.4 0.9 fusion.84
  2.3 6.8 %collective-permute-start = (f32[2,2,8,768]{3,2,1,0:T(8,128)S(1)}, f32[2,2,8,768]{3,2,1,0:T(8,128)S(1)}, u32[]{:S(2)}, u32[]{:S(2)}) collective-permute-start(f32[2,2,8,768]{3,2,1,0:T(8,128)S(1)} %pad_maximum_fusion.2), channel_id=1, source_target_pairs={{0,8},{8,16},{16,24},{24,32},{32,40},{40,48},{48,56},{56,64},{64,7... | collective-permute-start | bytes 294920 | tf_op jit(solution)/shard_map/ppermute | solution.py:111
  9.2 12.6 %collective-permute-start.1 = (f32[2,2,8,768]{3,2,1,0:T(8,128)S(1)}, f32[2,2,8,768]{3,2,1,0:T(8,128)S(1)}, u32[]{:S(2)}, u32[]{:S(2)}) collective-permute-start(f32[2,2,8,768]{3,2,1,0:T(8,128)S(1)} %pad_maximum_fusion.3), channel_id=1, source_target_pairs={{8,0},{16,8},{24,16},{32,24},{40,32},{48,40},{56,48},{64,56},{72,6... | collective-permute-start | bytes 294920 | tf_op jit(solution)/shard_map/ppermute | solution.py:112
  22.0 0.0 copy-done.2
  22.0 0.2 exponential_reduce_fusion
  22.2 12.3 %fusion.27 = (f32[8,384,128]{2,1,0:T(8,128)S(1)}, f32[8,384,128]{2,1,0:T(8,128)S(1)}, f32[8,384,128]{2,1,0:T(8,128)S(1)}, f32[8,384,128]{2,1,0:T(8,128)S(1)}, f3...) fusion(f32[384,128]{1,0:T(8,128)S(1)} %fusion.62, f32[384,128]{1,0:T(8,128)S(1)} %broadcast_multiply_fusion.1, ...), kind=kLoop, calls=%fused_computation.33 | loop fusion | flops 9830400 | bytes 10223680 | tf_op jit(solution)/shard_map/div | solution.py:37
  34.5 0.0 copy-start.1
  34.5 5.1 %maximum_maximum_fusion = (f32[8,768,256]{2,1,0:T(8,128)}, f32[8,768,256]{2,1,0:T(8,128)}) fusion(f32[8,384,128]{2,1,0:T(8,128)S(1)} %get-tuple-element.39, f32[8,384,128]{2,1,0:T(8,128)S(1)} %get-tuple-element.40, f32[8,384,128]{2,1,0:T(8,128)S(1)} %get-tuple-element.41, f32[8,384,128]{2,1,0:T(8,128)S(1)} %get-tuple-element.38, ...), kind=kLoop, calls=%fused_computation | loop fusion | flops 9437184 | bytes 22020096 | tf_op jit(solution)/shard_map/concatenate | solution.py:44
  39.7 0.0 collective-permute-done
  39.7 0.0 collective-permute-done.1
  39.7 0.0 copy-done.1
  39.8 0.1 copy.89
  39.9 0.1 copy.90
  40.1 0.1 copy.91
  40.2 0.3 maximum_bitcast_fusion
  40.5 0.6 reshape.320
  41.0 6.1 %multiply_reduce_fusion.3 = (f32[14,256]{1,0:T(8,128)S(1)}, f32[8,14,256]{2,1,0:T(8,128)S(1)}, f32[2,8,14,256]{3,2,0,1:T(8,128)S(1)}) fusion(f32[2,8,14,768]{3,1,2,0:T(8,128)S(1)} %reshape.320, f32[8,768,256]{2,1,0:T(8,128)} %get-tuple-element.4), kind=kOutput, calls=%fused_computation.56 | convolution fusion | flops 528679424 | bytes 7337984 | tf_op jit(solution)/shard_map/pcjq,cqn->pcjn/dot_general | solution.py:56
  47.1 0.1 bitcast_reduce_fusion
  47.2 2.5 %psum.77 = f32[1792]{0:T(1024)S(1)} all-reduce(f32[1792]{0:T(1024)S(1)} %bitcast.178), channel_id=1, replica_groups=mesh['z'=4,'x'=8,'yh'=2,'ylo'=4,'core'=2] {'core'}, use_global_device_ids=true, to_apply=%region_3.0 | all-reduce | flops 1792 | bytes 14336 | tf_op jit(solution)/shard_map/psum | solution.py:82
  49.8 9.9 %psum.78 = f32[1792]{0:T(1024)S(1)} all-reduce(f32[1792]{0:T(1024)S(1)} %psum.77), channel_id=1, replica_groups=mesh['z'=4,'x'=8,'yh'=2,'ylo'=4,'core'=2] {'ylo'}, use_global_device_ids=true, to_apply=%region_4.0 | all-reduce | flops 1792 | bytes 14336 | tf_op jit(solution)/shard_map/psum | solution.py:82
  59.7 0.1 copy_bitcast_fusion
  59.8 0.2 fusion.66
  60.1 0.2 fusion.55
  60.3 0.4 fusion.53
  60.7 0.5 reshape.321
  61.2 0.0 copy-start
  61.2 6.1 %multiply_reduce_fusion.1 = (f32[12,256]{1,0:T(8,128)S(1)}, f32[8,12,256]{2,1,0:T(8,128)S(1)}, f32[2,8,12,256]{3,2,0,1:T(8,128)S(1)}) fusion(f32[2,8,12,768]{3,1,2,0:T(8,128)S(1)} %reshape.321, f32[8,768,256]{2,1,0:T(8,128)} %get-tuple-element.4), kind=kOutput, calls=%fused_computation.54 | convolution fusion | flops 453153792 | bytes 7188480 | tf_op jit(solution)/shard_map/pcjq,cqn->pcjn/dot_general | solution.py:56
  67.3 0.1 bitcast_reduce_fusion.1
  67.4 2.5 %psum.79 = f32[1536]{0:T(1024)S(1)} all-reduce(f32[1536]{0:T(1024)S(1)} %bitcast.179), channel_id=1, replica_groups=mesh['z'=4,'x'=8,'yh'=2,'ylo'=4,'core'=2] {'core'}, use_global_device_ids=true, to_apply=%region_9.0 | all-reduce | flops 1536 | bytes 12288 | tf_op jit(solution)/shard_map/psum | solution.py:82
  69.9 9.4 %psum.80 = f32[1536]{0:T(1024)S(1)} all-reduce(f32[1536]{0:T(1024)S(1)} %psum.79), channel_id=1, replica_groups=mesh['z'=4,'x'=8,'yh'=2,'ylo'=4,'core'=2] {'ylo'}, use_global_device_ids=true, to_apply=%region_10.0 | all-reduce | flops 1536 | bytes 12288 | tf_op jit(solution)/shard_map/psum | solution.py:82
  79.3 0.1 copy_bitcast_fusion.2
  79.5 0.2 fusion.71
  79.7 0.0 copy-done
  79.7 0.2 multiply_reduce_fusion.10
  79.9 8.8 %psum.81 = f32[3,8]{1,0:T(4,128)S(1)} all-reduce(f32[3,8]{1,0:T(4,128)S(1)} %pad_maximum_fusion.4), channel_id=1, replica_groups=mesh['z'=4,'x'=8,'yh'=2,'ylo'=4,'core'=2] {'yh'}, use_global_device_ids=true, to_apply=%region_16.0 | all-reduce | flops 24 | bytes 192 | tf_op jit(solution)/shard_map/psum | solution.py:76
  88.7 16.0 %psum.82 = f32[3,8]{1,0:T(4,128)S(1)} all-reduce(f32[3,8]{1,0:T(4,128)S(1)} %psum.81), channel_id=1, replica_groups=mesh['z'=4,'x'=8,'yh'=2,'ylo'=4,'core'=2] {'x'}, use_global_device_ids=true, to_apply=%region_17.0 | all-reduce | flops 24 | bytes 192 | tf_op jit(solution)/shard_map/psum | solution.py:76
  104.7 14.3 %psum.83 = f32[3,8]{1,0:T(4,128)S(1)} all-reduce(f32[3,8]{1,0:T(4,128)S(1)} %psum.82), channel_id=1, replica_groups=mesh['z'=4,'x'=8,'yh'=2,'ylo'=4,'core'=2] {'z'}, use_global_device_ids=true, to_apply=%region_18.0 | all-reduce | flops 24 | bytes 192 | tf_op jit(solution)/shard_map/psum | solution.py:76
  119.1 0.1 multiply_reduce_fusion.5
  119.2 2.5 %psum.84 = f32[1536]{0:T(1024)S(1)} all-reduce(f32[1536]{0:T(1024)S(1)} %get-tuple-element.10), channel_id=1, replica_groups=mesh['z'=4,'x'=8,'yh'=2,'ylo'=4,'core'=2] {'core'}, use_global_device_ids=true, to_apply=%region_20.0 | all-reduce | flops 1536 | bytes 12288 | tf_op jit(solution)/shard_map/psum | solution.py:82
  121.7 8.5 %psum.85 = f32[1536]{0:T(1024)S(1)} all-reduce(f32[1536]{0:T(1024)S(1)} %psum.84), channel_id=1, replica_groups=mesh['z'=4,'x'=8,'yh'=2,'ylo'=4,'core'=2] {'ylo'}, use_global_device_ids=true, to_apply=%region_21.0 | all-reduce | flops 1536 | bytes 12288 | tf_op jit(solution)/shard_map/psum | solution.py:82
  130.3 0.2 fusion.69
  130.5 0.2 maximum_multiply_fusion
  130.7 0.1 fusion.82
  130.9 0.2 maximum_bitcast_fusion.1
  131.1 0.4 reshape.322
  131.5 6.0 %fusion.43 = f32[2,8,10,256]{3,2,0,1:T(8,128)S(1)} fusion(f32[8,768,256]{2,1,0:T(8,128)} %get-tuple-element.5, f32[2,8,10,768]{3,1,2,0:T(8,128)S(1)} %reshape.322), kind=kOutput, calls=%fused_computation.41 | convolution fusion | flops 377487360 | bytes 6946816 | tf_op jit(solution)/shard_map/pcjq,cqn->pcjn/dot_general | solution.py:56
  137.5 0.1 multiply_reduce_fusion.7
  137.6 2.5 %psum.86 = f32[1280]{0:T(1024)S(1)} all-reduce(f32[1280]{0:T(1024)S(1)} %bitcast.180), channel_id=1, replica_groups=mesh['z'=4,'x'=8,'yh'=2,'ylo'=4,'core'=2] {'core'}, use_global_device_ids=true, to_apply=%region_24.25 | all-reduce | flops 1280 | bytes 10240 | tf_op jit(solution)/shard_map/psum | solution.py:82
  140.1 10.5 %psum.87 = f32[1280]{0:T(1024)S(1)} all-reduce(f32[1280]{0:T(1024)S(1)} %psum.86), channel_id=1, replica_groups=mesh['z'=4,'x'=8,'yh'=2,'ylo'=4,'core'=2] {'ylo'}, use_global_device_ids=true, to_apply=%region_25.26 | all-reduce | flops 1280 | bytes 10240 | tf_op jit(solution)/shard_map/psum | solution.py:82
  150.6 0.2 fusion.74
  150.9 0.1 copy.85
  151.0 5.4 %fusion.46 = f32[2,2,8,8,128]{4,3,1,0,2:T(8,128)S(1)} fusion(f32[2,8,8,768]{3,2,0,1:T(8,128)S(1)} %bitcast.167, f32[8,768,256]{2,1,0:T(8,128)} %get-tuple-element.5), kind=kOutput, calls=%fused_computation.42 | convolution fusion | flops 301989888 | bytes 6815744 | tf_op jit(solution)/shard_map/pcjq,cqn->pcjn/dot_general | solution.py:56
  156.4 0.7 copy.115
  157.2 0.7 slice.152
  (33 shorter events, 0.6 us)
Async XLA Ops:
  0.6 21.4 %copy-start.2 = (s32[8]{0:T(128)S(1)}, s32[8]{0:T(128)}, u32[]{:S(2)}) copy-start(s32[8]{0:T(128)} %param.5) | copy-start | bytes 100
  2.3 37.3 %collective-permute-start = (f32[2,2,8,768]{3,2,1,0:T(8,128)S(1)}, f32[2,2,8,768]{3,2,1,0:T(8,128)S(1)}, u32[]{:S(2)}, u32[]{:S(2)}) collective-permute-start(f32[2,2,8,768]{3,2,1,0:T(8,128)S(1)} %pad_maximum_fusion.2), channel_id=1, source_target_pairs={{0,8},{8,16},{16,24},{24,32},{32,40},{40,48},{48,56},{56,64},{64,7... | collective-permute-start | bytes 294920 | tf_op jit(solution)/shard_map/ppermute | solution.py:111
  9.2 30.5 %collective-permute-start.1 = (f32[2,2,8,768]{3,2,1,0:T(8,128)S(1)}, f32[2,2,8,768]{3,2,1,0:T(8,128)S(1)}, u32[]{:S(2)}, u32[]{:S(2)}) collective-permute-start(f32[2,2,8,768]{3,2,1,0:T(8,128)S(1)} %pad_maximum_fusion.3), channel_id=1, source_target_pairs={{8,0},{16,8},{24,16},{32,24},{40,32},{48,40},{56,48},{64,56},{72,6... | collective-permute-start | bytes 294920 | tf_op jit(solution)/shard_map/ppermute | solution.py:112
  34.5 5.2 %copy-start.1 = (f32[2,2,8,1024]{3,2,1,0:T(8,128)S(1)}, f32[2,2,8,1024]{3,2,1,0:T(8,128)}, u32[]{:S(2)}) copy-start(f32[2,2,8,1024]{3,2,1,0:T(8,128)} %param.3) | copy-start | bytes 393220
  61.2 18.5 %copy-start = (f32[1,2,2,8,1024]{4,3,2,1,0:T(8,128)S(1)}, f32[1,2,2,8,1024]{4,3,2,1,0:T(8,128)}, u32[]{:S(2)}) copy-start(f32[1,2,2,8,1024]{4,3,2,1,0:T(8,128)} %param.4) | copy-start | bytes 393220
where the time goes:
time: 158 us
  blocking collectives  87.5 us (55%)
  matrix products  23.6 us (15%)
  other arithmetic  20.7 us (13%)
  starting transfers between devices  19.4 us (12%)
  local copies, waits for them, and re-layouts  5.48 us (3%)
    psum x8, blocking collectives, psum_chan(): value = lax.psum(value, axis)  48.4 us
    psum x3, blocking collectives, psum_tm(): value = lax.psum(value, axis)  39.1 us
    dot_general x4, matrix products, disperse(): jnp.einsum('pcjq,cqn->pcjn', stacked, table, precision=lax.Precision.HIGH...  23.6 us
    ppermute x1, starting transfers between devices, on_device(): after = lax.ppermute(leading, TM, down)  12.6 us
    div x1, other arithmetic, tap_tables(): mat_im = sign * interior_part * symbol_profile * jnp.sin(turn) / scale  12.3 us
    ppermute x1, starting transfers between devices, on_device(): before = lax.ppermute(trailing, TM, up)  6.83 us
    concatenate x1, other arithmetic, merged_table(): return jnp.concatenate([top, bottom], axis=1)  5.14 us
  transfers between devices with their start and end apart: 2, of which 0 were waited for; matrix products, arithmetic and copies ran while one was open for 11% of the time, Pallas kernels for 0%

commit v1 on v0

--- a/solution.py
+++ b/solution.py
@@ -2,6 +2,7 @@
 import jax.numpy as jnp
 from jax import lax
 from jax.sharding import Mesh, PartitionSpec as P
+from jax.lax import all_gather
 
 OPTICAL_CHANNELS = 64
 FILTER_HALF_TAPS = 128
@@ -79,7 +80,7 @@
 
 def psum_chan(value):
     for axis in ("core", "ylo"):
-        value = lax.psum(value, axis)
+        value = jnp.sum(all_gather(value, axis), axis=0)
     return value
 
 

time: 158 us -> 169 us (1.070)
  blocking collectives: 87.5 us -> 97.9 us
    all_gather x0 -> x8, blocking collectives: none -> 58.7 us  [psum_chan(): value = jnp.sum(all_gather(value, axis), axis=0)]
    psum x8 -> x0, blocking collectives: 48.4 us -> none  [psum_chan(): value = lax.psum(value, axis)]
where the time goes in v1:
time: 169 us
  blocking collectives  97.9 us (58%)
  matrix products  23.6 us (14%)
  other arithmetic  20.9 us (12%)
  starting transfers between devices  19.4 us (11%)
  local copies, waits for them, and re-layouts  5.55 us (3%)
    all_gather x8, blocking collectives, psum_chan(): value = jnp.sum(all_gather(value, axis), axis=0)  58.7 us
    psum x3, blocking collectives, psum_tm(): value = lax.psum(value, axis)  39.1 us
    dot_general x4, matrix products, disperse(): jnp.einsum('pcjq,cqn->pcjn', stacked, table, precision=lax.Precision.HIGH...  23.6 us
    ppermute x1, starting transfers between devices, on_device(): after = lax.ppermute(leading, TM, down)  12.6 us
    div x1, other arithmetic, tap_tables(): mat_im = sign * interior_part * symbol_profile * jnp.sin(turn) / scale  12.3 us
    ppermute x1, starting transfers between devices, on_device(): before = lax.ppermute(trailing, TM, up)  6.83 us
    concatenate x1, other arithmetic, merged_table(): return jnp.concatenate([top, bottom], axis=1)  5.14 us
  transfers between devices with their start and end apart: 2, of which 0 were waited for; matrix products, arithmetic and copies ran while one was open for 11% of the time, Pallas kernels for 0%

profile of v1, /device:TPU:8, one launch (start us, length us, event | category | flops | bytes accessed | tf_op | source)
XLA Modules:
  0.0 168.5 jit_solution(8352039086893406865)
XLA Ops:
  0.6 0.0 copy-start.2
  0.6 0.8 fusion.85
  1.4 0.9 fusion.84
  2.3 6.8 %collective-permute-start = (f32[2,2,8,768]{3,2,1,0:T(8,128)S(1)}, f32[2,2,8,768]{3,2,1,0:T(8,128)S(1)}, u32[]{:S(2)}, u32[]{:S(2)}) collective-permute-start(f32[2,2,8,768]{3,2,1,0:T(8,128)S(1)} %pad_maximum_fusion.2), channel_id=1, source_target_pairs={{0,8},{8,16},{16,24},{24,32},{32,40},{40,48},{48,56},{56,64},{64,7... | collective-permute-start | bytes 294920 | tf_op jit(solution)/shard_map/ppermute | solution.py:112
  9.2 12.6 %collective-permute-start.1 = (f32[2,2,8,768]{3,2,1,0:T(8,128)S(1)}, f32[2,2,8,768]{3,2,1,0:T(8,128)S(1)}, u32[]{:S(2)}, u32[]{:S(2)}) collective-permute-start(f32[2,2,8,768]{3,2,1,0:T(8,128)S(1)} %pad_maximum_fusion.3), channel_id=1, source_target_pairs={{8,0},{16,8},{24,16},{32,24},{40,32},{48,40},{56,48},{64,56},{72,6... | collective-permute-start | bytes 294920 | tf_op jit(solution)/shard_map/ppermute | solution.py:113
  22.0 0.0 copy-done.2
  22.0 0.2 exponential_reduce_fusion
  22.2 12.3 %fusion.27 = (f32[8,384,128]{2,1,0:T(8,128)S(1)}, f32[8,384,128]{2,1,0:T(8,128)S(1)}, f32[8,384,128]{2,1,0:T(8,128)S(1)}, f32[8,384,128]{2,1,0:T(8,128)S(1)}, f3...) fusion(f32[384,128]{1,0:T(8,128)S(1)} %fusion.62, f32[384,128]{1,0:T(8,128)S(1)} %broadcast_multiply_fusion.1, ...), kind=kLoop, calls=%fused_computation.33 | loop fusion | flops 9830400 | bytes 10223680 | tf_op jit(solution)/shard_map/div | solution.py:38
  34.5 0.0 copy-start.1
  34.5 5.1 %maximum_maximum_fusion = (f32[8,768,256]{2,1,0:T(8,128)}, f32[8,768,256]{2,1,0:T(8,128)}) fusion(f32[8,384,128]{2,1,0:T(8,128)S(1)} %get-tuple-element.39, f32[8,384,128]{2,1,0:T(8,128)S(1)} %get-tuple-element.40, f32[8,384,128]{2,1,0:T(8,128)S(1)} %get-tuple-element.41, f32[8,384,128]{2,1,0:T(8,128)S(1)} %get-tuple-element.38, ...), kind=kLoop, calls=%fused_computation | loop fusion | flops 9437184 | bytes 22020096 | tf_op jit(solution)/shard_map/concatenate | solution.py:45
  39.7 0.0 collective-permute-done
  39.7 0.0 collective-permute-done.1
  39.7 0.0 copy-done.1
  39.8 0.1 copy.89
  39.9 0.1 copy.90
  40.1 0.1 copy.91
  40.2 0.3 maximum_bitcast_fusion
  40.5 0.6 reshape.335
  41.0 6.1 %multiply_reduce_fusion.3 = (f32[14,256]{1,0:T(8,128)S(1)}, f32[8,14,256]{2,1,0:T(8,128)S(1)}, f32[2,8,14,256]{3,2,0,1:T(8,128)S(1)}) fusion(f32[2,8,14,768]{3,1,2,0:T(8,128)S(1)} %reshape.335, f32[8,768,256]{2,1,0:T(8,128)} %get-tuple-element.4), kind=kOutput, calls=%fused_computation.56 | convolution fusion | flops 528679424 | bytes 7337984 | tf_op jit(solution)/shard_map/pcjq,cqn->pcjn/dot_general | solution.py:57
  47.2 1.8 %all-gather.5 = f32[2,1,1792]{2,1,0:T(1,128)S(1)} all-gather(f32[1,1,1792]{2,1,0:T(1,128)S(1)} %reshape.348), channel_id=1, replica_groups=mesh['z'=4,'x'=8,'yh'=2,'ylo'=4,'core'=2] {'core'}, dimensions={0}, use_global_device_ids=true | all-gather | bytes 21504 | tf_op jit(solution)/shard_map/all_gather | solution.py:83
  49.1 11.7 %all-gather.6 = f32[4,1,1792]{2,1,0:T(1,128)S(1)} all-gather(f32[1,1,1792]{2,1,0:T(1,128)S(1)} %reshape.350), channel_id=2, replica_groups=mesh['z'=4,'x'=8,'yh'=2,'ylo'=4,'core'=2] {'ylo'}, dimensions={0}, use_global_device_ids=true | all-gather | bytes 35840 | tf_op jit(solution)/shard_map/all_gather | solution.py:83
  60.8 0.1 bitcast_reduce_fusion
  60.9 0.1 copy_bitcast_fusion
  61.1 0.2 fusion.66
  61.3 0.2 fusion.55
  61.6 0.4 fusion.53
  61.9 0.5 reshape.336
  62.4 6.1 %multiply_reduce_fusion.1 = (f32[12,256]{1,0:T(8,128)S(1)}, f32[8,12,256]{2,1,0:T(8,128)S(1)}, f32[2,8,12,256]{3,2,0,1:T(8,128)S(1)}) fusion(f32[2,8,12,768]{3,1,2,0:T(8,128)S(1)} %reshape.336, f32[8,768,256]{2,1,0:T(8,128)} %get-tuple-element.4), kind=kOutput, calls=%fused_computation.54 | convolution fusion | flops 453153792 | bytes 7188480 | tf_op jit(solution)/shard_map/pcjq,cqn->pcjn/dot_general | solution.py:57
  68.5 0.0 copy-start
  68.6 1.8 %all-gather.7 = f32[2,1,1536]{2,1,0:T(1,128)S(1)} all-gather(f32[1,1,1536]{2,1,0:T(1,128)S(1)} %reshape.352), channel_id=1, replica_groups=mesh['z'=4,'x'=8,'yh'=2,'ylo'=4,'core'=2] {'core'}, dimensions={0}, use_global_device_ids=true | all-gather | bytes 18432 | tf_op jit(solution)/shard_map/all_gather | solution.py:83
  70.4 13.2 %all-gather.8 = f32[4,1,1536]{2,1,0:T(1,128)S(1)} all-gather(f32[1,1,1536]{2,1,0:T(1,128)S(1)} %reshape.354), channel_id=3, replica_groups=mesh['z'=4,'x'=8,'yh'=2,'ylo'=4,'core'=2] {'ylo'}, dimensions={0}, use_global_device_ids=true | all-gather | bytes 30720 | tf_op jit(solution)/shard_map/all_gather | solution.py:83
  83.7 0.1 bitcast_reduce_fusion.1
  83.8 0.1 copy_bitcast_fusion.2
  83.9 0.2 fusion.71
  84.1 0.0 copy-done
  84.1 0.2 multiply_reduce_fusion.10
  84.3 8.8 %psum.21 = f32[3,8]{1,0:T(4,128)S(1)} all-reduce(f32[3,8]{1,0:T(4,128)S(1)} %pad_maximum_fusion.4), channel_id=1, replica_groups=mesh['z'=4,'x'=8,'yh'=2,'ylo'=4,'core'=2] {'yh'}, use_global_device_ids=true, to_apply=%region_16.0 | all-reduce | flops 24 | bytes 192 | tf_op jit(solution)/shard_map/psum | solution.py:77
  93.2 15.9 %psum.22 = f32[3,8]{1,0:T(4,128)S(1)} all-reduce(f32[3,8]{1,0:T(4,128)S(1)} %psum.21), channel_id=1, replica_groups=mesh['z'=4,'x'=8,'yh'=2,'ylo'=4,'core'=2] {'x'}, use_global_device_ids=true, to_apply=%region_17.0 | all-reduce | flops 24 | bytes 192 | tf_op jit(solution)/shard_map/psum | solution.py:77
  109.1 14.4 %psum.23 = f32[3,8]{1,0:T(4,128)S(1)} all-reduce(f32[3,8]{1,0:T(4,128)S(1)} %psum.22), channel_id=1, replica_groups=mesh['z'=4,'x'=8,'yh'=2,'ylo'=4,'core'=2] {'z'}, use_global_device_ids=true, to_apply=%region_18.0 | all-reduce | flops 24 | bytes 192 | tf_op jit(solution)/shard_map/psum | solution.py:77
  123.5 0.1 multiply_reduce_fusion.5
  123.7 1.8 %all-gather.9 = f32[2,1,1536]{2,1,0:T(1,128)S(1)} all-gather(f32[1,1,1536]{2,1,0:T(1,128)S(1)} %reshape.356), channel_id=4, replica_groups=mesh['z'=4,'x'=8,'yh'=2,'ylo'=4,'core'=2] {'core'}, dimensions={0}, use_global_device_ids=true | all-gather | bytes 18432 | tf_op jit(solution)/shard_map/all_gather | solution.py:83
  125.5 13.2 %all-gather.10 = f32[4,1,1536]{2,1,0:T(1,128)S(1)} all-gather(f32[1,1,1536]{2,1,0:T(1,128)S(1)} %reshape.358), channel_id=5, replica_groups=mesh['z'=4,'x'=8,'yh'=2,'ylo'=4,'core'=2] {'ylo'}, dimensions={0}, use_global_device_ids=true | all-gather | bytes 30720 | tf_op jit(solution)/shard_map/all_gather | solution.py:83
  138.8 0.2 fusion.69
  139.0 0.2 maximum_multiply_fusion
  139.2 0.1 fusion.82
  139.4 0.2 maximum_bitcast_fusion.1
  139.6 0.4 reshape.337
  140.0 6.0 %fusion.43 = f32[2,8,10,256]{3,2,0,1:T(8,128)S(1)} fusion(f32[8,768,256]{2,1,0:T(8,128)} %get-tuple-element.5, f32[2,8,10,768]{3,1,2,0:T(8,128)S(1)} %reshape.337), kind=kOutput, calls=%fused_computation.41 | convolution fusion | flops 377487360 | bytes 6946816 | tf_op jit(solution)/shard_map/pcjq,cqn->pcjn/dot_general | solution.py:57
  146.0 0.1 multiply_reduce_fusion.7
  146.1 1.8 %all-gather.11 = f32[2,1,1280]{2,1,0:T(1,128)S(1)} all-gather(f32[1,1,1280]{2,1,0:T(1,128)S(1)} %reshape.360), channel_id=1, replica_groups=mesh['z'=4,'x'=8,'yh'=2,'ylo'=4,'core'=2] {'core'}, dimensions={0}, use_global_device_ids=true | all-gather | bytes 15360 | tf_op jit(solution)/shard_map/all_gather | solution.py:83
  148.0 13.3 %all-gather.12 = f32[4,1,1280]{2,1,0:T(1,128)S(1)} all-gather(f32[1,1,1280]{2,1,0:T(1,128)S(1)} %reshape.362), channel_id=6, replica_groups=mesh['z'=4,'x'=8,'yh'=2,'ylo'=4,'core'=2] {'ylo'}, dimensions={0}, use_global_device_ids=true | all-gather | bytes 25600 | tf_op jit(solution)/shard_map/all_gather | solution.py:83
  161.3 0.2 fusion.74
  161.6 0.1 copy.85
  161.7 5.4 %fusion.46 = f32[2,2,8,8,128]{4,3,1,0,2:T(8,128)S(1)} fusion(f32[2,8,8,768]{3,2,0,1:T(8,128)S(1)} %bitcast.164, f32[8,768,256]{2,1,0:T(8,128)} %get-tuple-element.5), kind=kOutput, calls=%fused_computation.42 | convolution fusion | flops 301989888 | bytes 6815744 | tf_op jit(solution)/shard_map/pcjq,cqn->pcjn/dot_general | solution.py:57
  167.1 0.7 copy.115
  167.9 0.7 slice.152
  (49 shorter events, 0.9 us)
Async XLA Ops:
  0.6 21.4 %copy-start.2 = (s32[8]{0:T(128)S(1)}, s32[8]{0:T(128)}, u32[]{:S(2)}) copy-start(s32[8]{0:T(128)} %param.5) | copy-start | bytes 100
  2.3 37.3 %collective-permute-start = (f32[2,2,8,768]{3,2,1,0:T(8,128)S(1)}, f32[2,2,8,768]{3,2,1,0:T(8,128)S(1)}, u32[]{:S(2)}, u32[]{:S(2)}) collective-permute-start(f32[2,2,8,768]{3,2,1,0:T(8,128)S(1)} %pad_maximum_fusion.2), channel_id=1, source_target_pairs={{0,8},{8,16},{16,24},{24,32},{32,40},{40,48},{48,56},{56,64},{64,7... | collective-permute-start | bytes 294920 | tf_op jit(solution)/shard_map/ppermute | solution.py:112
  9.2 30.5 %collective-permute-start.1 = (f32[2,2,8,768]{3,2,1,0:T(8,128)S(1)}, f32[2,2,8,768]{3,2,1,0:T(8,128)S(1)}, u32[]{:S(2)}, u32[]{:S(2)}) collective-permute-start(f32[2,2,8,768]{3,2,1,0:T(8,128)S(1)} %pad_maximum_fusion.3), channel_id=1, source_target_pairs={{8,0},{16,8},{24,16},{32,24},{40,32},{48,40},{56,48},{64,56},{72,6... | collective-permute-start | bytes 294920 | tf_op jit(solution)/shard_map/ppermute | solution.py:113
  34.5 5.2 %copy-start.1 = (f32[2,2,8,1024]{3,2,1,0:T(8,128)S(1)}, f32[2,2,8,1024]{3,2,1,0:T(8,128)}, u32[]{:S(2)}) copy-start(f32[2,2,8,1024]{3,2,1,0:T(8,128)} %param.3) | copy-start | bytes 393220
  68.5 15.6 %copy-start = (f32[1,2,2,8,1024]{4,3,2,1,0:T(8,128)S(1)}, f32[1,2,2,8,1024]{4,3,2,1,0:T(8,128)}, u32[]{:S(2)}) copy-start(f32[1,2,2,8,1024]{4,3,2,1,0:T(8,128)} %param.4) | copy-start | bytes 393220
